TPU v7x, 512 devices: a whole 4x4x16 slice. The times are simulated.
512 devices in a mesh: row: 32 (over x, y, core), col: 16 (over z).
Axes of the slice: x: 4, y: 4, z: 16, core: 2. Of those that a mesh axis runs over, the one named last changes fastest.
Arguments:
- panel: float32 [65536, 256], P('row', 'col'), may hold values from -210 to 210
- slab: float32 [65536, 4096], P('row', 'col'), may hold values from -6 to 6
Outputs:
- triangle: float32 [256, 256], P(None, 'col')
- projected: float32 [256, 4096], P(None, 'col')
- residual: float32 [65536, 4096], P('row', 'col')
All inputs are finite; a program needn't handle non-finite values.
Results may differ from a plain program's by a relative error of at most 0.0003.
Values sent between devices are 32-bit elements; how exact they have to be, the bound alone decides.
No kernel may reach another device: no remote copies, remote signals or barrier semaphores. Data moves between devices by JAX's collectives and lax.ppermute only.
A program may use at most 64 MiB of HBM per device.

v0:
```python
import math
import jax
import jax.numpy as jnp
from jax import lax
from jax.sharding import PartitionSpec as P

contract_rows = (((0,), (0,)), ((), ()))


def per_device(panel, slab):
    highest = lax.Precision.HIGHEST
    gathered = lax.all_gather(panel, "col", axis=1, tiled=True)
    cross_local = lax.dot_general(gathered, slab, contract_rows, precision=highest)
    gram_local = lax.dot_general(gathered, gathered, contract_rows, precision=highest)
    gram_total, totals = lax.psum((gram_local, cross_local), "row")
    lower_factor = jnp.linalg.cholesky(gram_total)
    projected = lax.linalg.triangular_solve(
        lower_factor, totals, left_side=True, lower=True, transpose_a=False
    )
    basis_rows = lax.linalg.triangular_solve(
        lower_factor, gathered, left_side=False, lower=True, transpose_a=True
    )
    residual = slab - jnp.dot(basis_rows, projected, precision=highest)
    col_width = panel.shape[1]
    rows_total = gathered.shape[0] * lax.axis_size("row")
    scaled = lower_factor.T * (1.0 / math.sqrt(rows_total))
    triangle = lax.dynamic_slice_in_dim(scaled, lax.axis_index("col") * col_width, col_width, 1)
    return (triangle, projected, residual)


def solution(mesh):
    placed = (P("row", "col"), P("row", "col"))
    return jax.shard_map(
        per_device,
        mesh=mesh,
        in_specs=placed,
        out_specs=(P(None, "col"), P(None, "col"), P("row", "col")),
        check_vma=False,
    )
```

profile of v0, /device:TPU:1, one launch (start us, length us, event | category | flops | bytes accessed | tf_op | source)
XLA Modules:
  0.0 307.3 jit_solution(13206898415730622074)
XLA Ops:
  7.2 0.0 all-gather.2.cloned.1.call-start
  7.2 0.7 all-gather.2.cloned.1.call-update
  7.9 0.0 all-reduce.4.cloned.1.call-start
  7.9 71.5 %all-gather.2.cloned.1.call-done = f32[2048,256]{0,1:T(8,128)} async-done(((f32[2048,16]{0,1:T(8,128)}), f32[2048,256]{0,1:T(8,128)}) %all-gather.2.cloned.1.call-update) | async-done | bytes 2097168 | tf_op jit(solution)/shard_map/all_gather | solution.py:12
  79.5 0.0 copy-start
  79.5 4.9 %fusion.19 = f32[256,256]{0,1:T(8,128)} fusion(f32[2048,256]{0,1:T(8,128)} %all-gather.2.cloned.1.call-done), kind=kOutput, calls=%fused_computation.42 | convolution fusion | flops 1610612736 | bytes 2359296 | tf_op jit(solution)/shard_map/dot_general | solution.py:14
  84.4 0.0 copy-done
  84.4 4.2 %fusion.20 = f32[256,256]{1,0:T(8,128)} fusion(f32[2048,256]{0,1:T(8,128)S(1)} %copy-done, f32[2048,256]{1,0:T(8,128)} %param.3), kind=kOutput, calls=%fused_computation.43 | convolution fusion | flops 1610612736 | bytes 4456448 | tf_op jit(solution)/shard_map/dot_general | solution.py:13
  88.6 0.0 all-reduce.4.cloned.1.call-update
  88.6 140.3 %all-reduce.4.cloned.1.call-done = (f32[256,256]{0,1:T(8,128)}, f32[256,256]{1,0:T(8,128)}) async-done(((f32[256,256]{0,1:T(8,128)}, f32[256,256]{1,0:T(8,128)}), (f32[256,256]{0,1:T(8,128)}, f32[256,256]{1,0:T(8,128)})) %all-reduce.4.cloned.1.call-update) | async-done | bytes 524304 | tf_op jit(solution)/shard_map/psum | solution.py:15
  228.9 0.0 copy-start.3
  228.9 1.1 copy.6
  230.1 1.0 fusion.5
  231.1 11.7 %cholesky.50 = f32[128,128]{1,0:T(8,128)S(1)} custom-call(f32[128,128]{1,0:T(8,128)S(1)} %cholesky.118), custom_call_target="Cholesky" | custom-call | tf_op jit(solution)/shard_map/jit(cholesky)/cholesky | solution.py:16
  242.8 9.8 %custom-call.16 = f32[1,128,128]{1,2,0:T(8,128)S(1)} custom-call(f32[1,128,128]{2,1,0:T(8,128)S(1)} %get-tuple-element.28), custom_call_target="InvertDiagBlocksLowerTriangular" | custom-call | tf_op jit(solution)/shard_map/jit(cholesky)/cholesky | solution.py:16
  252.7 0.2 constant_dynamic-update-slice_fusion
  252.9 0.3 convolution_subtract_fusion.3
  253.2 11.9 %cholesky.105 = f32[128,128]{1,0:T(8,128)S(1)} custom-call(f32[128,128]{1,0:T(8,128)S(1)} %convolution_subtract_fusion.3), custom_call_target="Cholesky" | custom-call | tf_op jit(solution)/shard_map/jit(cholesky)/cholesky | solution.py:16
  265.1 0.6 compare_reduce_fusion
  267.1 0.1 triangular_solve.59
  267.1 4.0 %while.1 = (s32[]{:T(128)}, f32[256,256]{1,0:T(8,128)S(1)}, s32[2,2]{1,0:T(2,128)S(1)}, f32[2,128,128]{2,1,0:T(8,128)S(1)}, s32[]{:T(128)}) while((s32[]{:T(128)}, f32[256,256]{1,0:T(8,128)S(1)}, s32[2,2]{1,0:T(2,128)S(1)}, f32[2,128,128]{2,1,0:T(8,128)S(1)}, s32[]{:T(128)}) %tuple.28), condition=%wide.while_cond, body=%wide.while_body.sunk | while | flops 2 | bytes 131189 | solution.py:17
  267.1 0.6 fusion.33
  267.7 1.4 bitcast_dynamic-update-slice_fusion.2
  269.1 0.6 fusion.33
  269.7 1.4 bitcast_dynamic-update-slice_fusion.2
  271.1 19.7 %custom-call.17 = f32[2,128,128]{1,2,0:T(8,128)S(1)} custom-call(f32[2,128,128]{2,1,0:T(8,128)S(1)} %get-tuple-element.10), custom_call_target="InvertDiagBlocksLowerTriangular" | custom-call | tf_op jit(solution)/shard_map/triangular_solve | solution.py:17
  290.8 0.0 copy-done.3
  290.8 0.3 fusion.7
  291.1 0.3 convolution_subtract_fusion.2
  291.4 0.3 fusion.13
  291.8 0.0 copy-start.2
  291.8 1.0 fusion.3
  292.8 0.0 copy-start.1
  292.8 1.1 convolution_subtract_fusion.1
  293.9 1.1 fusion.12
  295.0 0.6 fusion.16
  295.6 0.0 copy-done.2
  295.6 0.0 copy-done.1
  295.6 4.9 %convolution_subtract_fusion = f32[2048,256]{1,0:T(8,128)} fusion(f32[2048,256]{1,0:T(8,128)S(1)} %copy-done.1, f32[256,256]{1,0:T(8,128)S(1)} %pad_maximum_fusion, f32[2048,128]{0,1:T(8,128)S(1)} %fusion.12, f32[2048,128]{0,1:T(8,128)S(1)} %bitcast.43), kind=kOutput, calls=%fused_computation.2 | convolution fusion | flops 1611661312 | bytes 6553600 | tf_op jit(solution)/shard_map/dot_general | solution.py:23
  (10 shorter events, 0.2 us)
Async XLA Ops:
  7.2 72.3 %all-gather.2.cloned.1.call-start = ((), (), s32[]{:S(2)}) async-start(), calls=%async_computation | async-start | bytes 2228224 | tf_op jit(solution)/shard_map/all_gather | solution.py:12
  7.9 221.0 %all-reduce.4.cloned.1.call-start = ((), (), s32[]{:S(2)}) async-start(), calls=%async_computation.1 | async-start | bytes 1048576 | tf_op jit(solution)/shard_map/psum | solution.py:15
  79.5 4.9 %copy-start = (f32[2048,256]{0,1:T(8,128)S(1)}, f32[2048,256]{0,1:T(8,128)}, u32[]{:S(2)}) copy-start(f32[2048,256]{0,1:T(8,128)} %all-gather.2.cloned.1.call-done) | copy-start | bytes 6291460
  228.9 61.9 %copy-start.3 = (f32[256,256]{1,0:T(8,128)S(1)}, f32[256,256]{1,0:T(8,128)}, u32[]{:S(2)}) copy-start(f32[256,256]{1,0:T(8,128)} %get-tuple-element.20) | copy-start | bytes 786436
  291.8 3.9 %copy-start.2 = (f32[256,256]{1,0:T(8,128)}, f32[256,256]{1,0:T(8,128)S(1)}, u32[]{:S(2)}) copy-start(f32[256,256]{1,0:T(8,128)S(1)} %pad_maximum_fusion) | copy-start | bytes 786436
  292.8 2.8 copy-start.1
Sparse Core Ops, SparseCore 0:
  10.1 69.3 all-gather.1
  88.7 140.1 all-reduce.3
where the time goes:
time: 308 us; the launch traced here: 307 us
  waiting for transfers between devices  213 us (69%)
  other arithmetic  55.5 us (18%)
  matrix products  18.5 us (6%)
  between operations  15.5 us (5%)
  local copies, waits for them, and re-layouts  5.19 us (2%)
    psum x1, waiting for transfers between devices, per_device(): gram_total, totals = lax.psum((gram_local, cross_local), 'row')  140 us
    all_gather x1, waiting for transfers between devices, per_device(): gathered = lax.all_gather(panel, 'col', axis=1, tiled=True)  71.5 us
    another operation x6, other arithmetic, per_device(): lower_factor = jnp.linalg.cholesky(gram_total)  34.1 us
    another operation x4, other arithmetic, per_device(): lax.linalg.triangular_solve(lower_factor, totals, left_side=True, lower=T...  19.7 us
  transfers between devices with their start and end apart: 2, of which 2 were waited for; matrix products, arithmetic and copies ran while one was open for 0% of the time, Pallas kernels for 0%

commit v1 on v0

--- a/solution.py
+++ b/solution.py
@@ -9,7 +9,22 @@
 
 def per_device(panel, slab):
     highest = lax.Precision.HIGHEST
-    gathered = lax.all_gather(panel, "col", axis=1, tiled=True)
+    ways, here, step = (lax.axis_size("col"), lax.axis_index("col"), panel.shape[1])
+    shape = [n * ways if d == 1 else n for d, n in enumerate(panel.shape)]
+    gathered = lax.dynamic_update_slice_in_dim(
+        jnp.zeros(shape, panel.dtype), panel, here * step, axis=1
+    )
+    going_up = going_down = panel
+    for far in range(1, ways // 2 + 1):
+        going_up = lax.ppermute(going_up, "col", [(d, (d + 1) % ways) for d in range(ways)])
+        gathered = lax.dynamic_update_slice_in_dim(
+            gathered, going_up, (here - far) % ways * step, axis=1
+        )
+        if 2 * far < ways:
+            going_down = lax.ppermute(going_down, "col", [(d, (d - 1) % ways) for d in range(ways)])
+            gathered = lax.dynamic_update_slice_in_dim(
+                gathered, going_down, (here + far) % ways * step, axis=1
+            )
     cross_local = lax.dot_general(gathered, slab, contract_rows, precision=highest)
     gram_local = lax.dot_general(gathered, gathered, contract_rows, precision=highest)
     gram_total, totals = lax.psum((gram_local, cross_local), "row")

time: 308 us -> 298 us (0.968)
  waiting for transfers between devices: 213 us -> 151 us
  starting transfers between devices: 0.08 us -> 54.7 us
  matrix products: 18.5 us -> 14.7 us
    all_gather x1 -> x0, waiting for transfers between devices: 71.5 us -> none  [per_device(): gathered = lax.all_gather(panel, 'col', axis=1, tiled=True)]
    ppermute x0 -> x15, starting transfers between devices: none -> 54.7 us  [the longest x7 36.9 us: per_device(): lax.ppermute(going_down, 'col', [(d, (d - 1) % ways) for d in range(ways)])]
    ppermute x0 -> x15, waiting for transfers between devices: none -> 9.91 us  [the longest x8 9.9 us: per_device(): lax.ppermute(going_up, 'col', [(d, (d + 1) % ways) for d in range(ways)])]
  transfers between devices with their start and end apart: 2 -> 16, of which waited for: 2 -> 9; matrix products, arithmetic and copies ran while one was open for 0% -> 0% of each run, Pallas kernels for 0% -> 0%
where the time goes in v1:
time: 298 us
  waiting for transfers between devices  151 us (51%)
  other arithmetic  55.5 us (19%)
  starting transfers between devices  54.7 us (18%)
  between operations  16.1 us (5%)
  matrix products  14.7 us (5%)
  local copies, waits for them, and re-layouts  6.08 us (2%)
    psum x1, waiting for transfers between devices, per_device(): gram_total, totals = lax.psum((gram_local, cross_local), 'row')  141 us
    ppermute x7, starting transfers between devices, per_device(): lax.ppermute(going_down, 'col', [(d, (d - 1) % ways) for d in range(ways)])  36.9 us
    another operation x6, other arithmetic, per_device(): lower_factor = jnp.linalg.cholesky(gram_total)  34.1 us
    another operation x4, other arithmetic, per_device(): lax.linalg.triangular_solve(lower_factor, totals, left_side=True, lower=T...  19.7 us
    ppermute x8, starting transfers between devices, per_device(): lax.ppermute(going_up, 'col', [(d, (d + 1) % ways) for d in range(ways)])  17.7 us
    ppermute x8, waiting for transfers between devices, per_device(): lax.ppermute(going_up, 'col', [(d, (d + 1) % ways) for d in range(ways)])  9.9 us
  transfers between devices with their start and end apart: 16, of which 9 were waited for; matrix products, arithmetic and copies ran while one was open for 0% of the time, Pallas kernels for 0%

profile of v1, /device:TPU:1, one launch (start us, length us, event | category | flops | bytes accessed | tf_op | source)
XLA Modules:
  0.0 297.7 jit_solution(11310904592474972377)
XLA Ops:
  7.2 0.0 copy-start.4
  7.2 0.0 all-reduce.4.cloned.1.call-start
  7.2 4.4 %collective-permute-start = (f32[2048,16]{0,1:T(8,128)}, f32[2048,16]{0,1:T(8,128)S(1)}, u32[]{:S(2)}, u32[]{:S(2)}) collective-permute-start(f32[2048,16]{0,1:T(8,128)} %param.2), channel_id=1, source_target_pairs={{0,1},{1,2},{2,3},{3,4},{4,5},{5,6},{6,7},{7,8},{8,9},{9,10},{10,1... | collective-permute-start | bytes 393224 | tf_op jit(solution)/shard_map/ppermute | solution.py:19
  11.6 9.5 %collective-permute-start.1 = (f32[2048,16]{0,1:T(8,128)}, f32[2048,16]{0,1:T(8,128)S(1)}, u32[]{:S(2)}, u32[]{:S(2)}) collective-permute-start(f32[2048,16]{0,1:T(8,128)} %param.2), channel_id=1, source_target_pairs={{0,15},{1,0},{2,1},{3,2},{4,3},{5,4},{6,5},{7,6},{8,7},{9,8},{10,9... | collective-permute-start | bytes 393224 | tf_op jit(solution)/shard_map/ppermute | solution.py:24
  21.4 0.2 broadcast_in_dim.5
  21.7 0.9 collective-permute-done
  22.6 1.9 collective-permute-start.2
  24.5 0.0 collective-permute-done.1
  24.5 4.6 %collective-permute-start.3 = (f32[2048,16]{0,1:T(8,128)S(1)}, f32[2048,16]{0,1:T(8,128)S(1)}, u32[]{:S(2)}, u32[]{:S(2)}) collective-permute-start(f32[2048,16]{0,1:T(8,128)S(1)} %collective-permute-done.1), channel_id=1, source_target_pairs={{0,15},{1,0},{2,1},{3,2},{4,3},{5,4},{6,5},{7,6},{8,7},{9,8},{10,9... | collective-permute-start | bytes 393224 | tf_op jit(solution)/shard_map/ppermute | solution.py:24
  29.2 0.4 collective-permute-done.2
  29.5 1.9 collective-permute-start.4
  31.4 0.0 collective-permute-done.3
  31.4 4.6 %collective-permute-start.5 = (f32[2048,16]{0,1:T(8,128)S(1)}, f32[2048,16]{0,1:T(8,128)S(1)}, u32[]{:S(2)}, u32[]{:S(2)}) collective-permute-start(f32[2048,16]{0,1:T(8,128)S(1)} %collective-permute-done.3), channel_id=1, source_target_pairs={{0,15},{1,0},{2,1},{3,2},{4,3},{5,4},{6,5},{7,6},{8,7},{9,8},{10,9... | collective-permute-start | bytes 393224 | tf_op jit(solution)/shard_map/ppermute | solution.py:24
  36.1 0.4 collective-permute-done.4
  36.4 1.9 collective-permute-start.6
  38.3 0.0 collective-permute-done.5
  38.3 4.6 %collective-permute-start.7 = (f32[2048,16]{0,1:T(8,128)S(1)}, f32[2048,16]{0,1:T(8,128)S(1)}, u32[]{:S(2)}, u32[]{:S(2)}) collective-permute-start(f32[2048,16]{0,1:T(8,128)S(1)} %collective-permute-done.5), channel_id=1, source_target_pairs={{0,15},{1,0},{2,1},{3,2},{4,3},{5,4},{6,5},{7,6},{8,7},{9,8},{10,9... | collective-permute-start | bytes 393224 | tf_op jit(solution)/shard_map/ppermute | solution.py:24
  43.0 0.4 collective-permute-done.6
  43.3 1.9 collective-permute-start.8
  45.2 0.0 collective-permute-done.7
  45.3 4.6 %collective-permute-start.9 = (f32[2048,16]{0,1:T(8,128)S(1)}, f32[2048,16]{0,1:T(8,128)S(1)}, u32[]{:S(2)}, u32[]{:S(2)}) collective-permute-start(f32[2048,16]{0,1:T(8,128)S(1)} %collective-permute-done.7), channel_id=1, source_target_pairs={{0,15},{1,0},{2,1},{3,2},{4,3},{5,4},{6,5},{7,6},{8,7},{9,8},{10,9... | collective-permute-start | bytes 393224 | tf_op jit(solution)/shard_map/ppermute | solution.py:24
  49.9 0.4 collective-permute-done.8
  50.2 1.9 collective-permute-start.10
  52.2 0.0 collective-permute-done.9
  52.2 4.6 %collective-permute-start.11 = (f32[2048,16]{0,1:T(8,128)S(1)}, f32[2048,16]{0,1:T(8,128)S(1)}, u32[]{:S(2)}, u32[]{:S(2)}) collective-permute-start(f32[2048,16]{0,1:T(8,128)S(1)} %collective-permute-done.9), channel_id=1, source_target_pairs={{0,15},{1,0},{2,1},{3,2},{4,3},{5,4},{6,5},{7,6},{8,7},{9,8},{10,9... | collective-permute-start | bytes 393224 | tf_op jit(solution)/shard_map/ppermute | solution.py:24
  56.8 0.4 collective-permute-done.10
  57.2 1.9 collective-permute-start.12
  59.1 0.0 collective-permute-done.11
  59.1 4.6 %collective-permute-start.13 = (f32[2048,16]{0,1:T(8,128)S(1)}, f32[2048,16]{0,1:T(8,128)S(1)}, u32[]{:S(2)}, u32[]{:S(2)}) collective-permute-start(f32[2048,16]{0,1:T(8,128)S(1)} %collective-permute-done.11), channel_id=1, source_target_pairs={{0,15},{1,0},{2,1},{3,2},{4,3},{5,4},{6,5},{7,6},{8,7},{9,8},{10,9... | collective-permute-start | bytes 393224 | tf_op jit(solution)/shard_map/ppermute | solution.py:24
  63.7 1.1 collective-permute-done.12
  64.8 1.9 collective-permute-start.14
  66.8 0.0 collective-permute-done.13
  66.8 6.1 %collective-permute-done.14 = f32[2048,16]{0,1:T(8,128)S(1)} collective-permute-done((f32[2048,16]{0,1:T(8,128)S(1)}, f32[2048,16]{0,1:T(8,128)S(1)}, u32[]{:S(2)}, u32[]{:S(2)}) %collective-permute-start.14) | collective-permute-done | bytes 131104 | tf_op jit(solution)/shard_map/ppermute | solution.py:19
  72.9 0.0 copy-start
  72.9 2.6 fusion.21
  75.5 2.6 fusion.22
  78.1 0.0 all-reduce.4.cloned.1.call-update
  78.1 140.6 %all-reduce.4.cloned.1.call-done = (f32[256,256]{0,1:T(8,128)}, f32[256,256]{1,0:T(8,128)}) async-done(((f32[256,256]{0,1:T(8,128)}, f32[256,256]{1,0:T(8,128)}), (f32[256,256]{0,1:T(8,128)}, f32[256,256]{1,0:T(8,128)})) %all-reduce.4.cloned.1.call-update) | async-done | bytes 524304 | tf_op jit(solution)/shard_map/psum | solution.py:30
  218.8 1.1 copy.6
  219.9 1.0 fusion.6
  220.9 11.7 %cholesky.50 = f32[128,128]{1,0:T(8,128)S(1)} custom-call(f32[128,128]{1,0:T(8,128)S(1)} %cholesky.118), custom_call_target="Cholesky" | custom-call | tf_op jit(solution)/shard_map/jit(cholesky)/cholesky | solution.py:31
  232.7 9.8 %custom-call.16 = f32[1,128,128]{1,2,0:T(8,128)S(1)} custom-call(f32[1,128,128]{2,1,0:T(8,128)S(1)} %get-tuple-element.28), custom_call_target="InvertDiagBlocksLowerTriangular" | custom-call | tf_op jit(solution)/shard_map/jit(cholesky)/cholesky | solution.py:31
  242.5 0.2 constant_dynamic-update-slice_fusion
  242.7 0.3 convolution_subtract_fusion.1
  243.0 11.9 %cholesky.105 = f32[128,128]{1,0:T(8,128)S(1)} custom-call(f32[128,128]{1,0:T(8,128)S(1)} %convolution_subtract_fusion.1), custom_call_target="Cholesky" | custom-call | tf_op jit(solution)/shard_map/jit(cholesky)/cholesky | solution.py:31
  254.9 0.6 compare_reduce_fusion
  256.9 0.6 fusion.18
  257.5 0.1 triangular_solve.57
  257.6 4.0 %while.1 = (s32[]{:T(128)}, f32[256,256]{1,0:T(8,128)S(1)}, s32[2,2]{1,0:T(2,128)S(1)}, f32[2,128,128]{2,1,0:T(8,128)S(1)}, s32[]{:T(128)}) while((s32[]{:T(128)}, f32[256,256]{1,0:T(8,128)S(1)}, s32[2,2]{1,0:T(2,128)S(1)}, f32[2,128,128]{2,1,0:T(8,128)S(1)}, s32[]{:T(128)}) %tuple.28), condition=%wide.while_cond, body=%wide.while_body.sunk | while | flops 2 | bytes 131189 | solution.py:32
  257.6 0.6 fusion.33
  258.1 1.4 bitcast_dynamic-update-slice_fusion.2
  259.6 0.6 fusion.33
  260.1 1.4 bitcast_dynamic-update-slice_fusion.2
  261.5 19.7 %custom-call.17 = f32[2,128,128]{1,2,0:T(8,128)S(1)} custom-call(f32[2,128,128]{2,1,0:T(8,128)S(1)} %get-tuple-element.10), custom_call_target="InvertDiagBlocksLowerTriangular" | custom-call | tf_op jit(solution)/shard_map/triangular_solve | solution.py:32
  281.2 1.1 fusion.4
  282.3 0.3 fusion.9
  282.6 0.3 fusion.16
  282.9 0.3 fusion.8
  283.3 0.0 copy-start.2
  283.3 1.1 fusion.14
  284.3 0.0 copy-start.1
  284.4 1.1 fusion.3
  285.5 0.4 copy-done.1
  285.9 4.9 %convolution_subtract_fusion = f32[2048,256]{1,0:T(8,128)} fusion(f32[2048,256]{1,0:T(8,128)S(1)} %copy-done.1, f32[256,256]{1,0:T(8,128)S(1)} %pad_maximum_fusion, f32[2048,128]{0,1:T(8,128)S(1)} %fusion.3, f32[2048,128]{0,1:T(8,128)S(1)} %fusion.4), kind=kOutput, calls=%fused_computation.2 | convolution fusion | flops 1611661312 | bytes 6553600 | tf_op jit(solution)/shard_map/dot_general | solution.py:38
  (31 shorter events, 0.4 us)
Async XLA Ops:
  7.2 14.5 %copy-start.4 = (f32[2048,16]{0,1:T(8,128)S(1)}, f32[2048,16]{0,1:T(8,128)}, u32[]{:S(2)}) copy-start(f32[2048,16]{0,1:T(8,128)} %param.2) | copy-start | bytes 393220
  7.2 211.6 %all-reduce.4.cloned.1.call-start = ((), (), s32[]{:S(2)}) async-start(), calls=%async_computation | async-start | bytes 1048576 | tf_op jit(solution)/shard_map/psum | solution.py:30
  7.2 15.4 %collective-permute-start = (f32[2048,16]{0,1:T(8,128)}, f32[2048,16]{0,1:T(8,128)S(1)}, u32[]{:S(2)}, u32[]{:S(2)}) collective-permute-start(f32[2048,16]{0,1:T(8,128)} %param.2), channel_id=1, source_target_pairs={{0,1},{1,2},{2,3},{3,4},{4,5},{5,6},{6,7},{7,8},{8,9},{9,10},{10,1... | collective-permute-start | bytes 393224 | tf_op jit(solution)/shard_map/ppermute | solution.py:19
  11.6 12.9 %collective-permute-start.1 = (f32[2048,16]{0,1:T(8,128)}, f32[2048,16]{0,1:T(8,128)S(1)}, u32[]{:S(2)}, u32[]{:S(2)}) collective-permute-start(f32[2048,16]{0,1:T(8,128)} %param.2), channel_id=1, source_target_pairs={{0,15},{1,0},{2,1},{3,2},{4,3},{5,4},{6,5},{7,6},{8,7},{9,8},{10,9... | collective-permute-start | bytes 393224 | tf_op jit(solution)/shard_map/ppermute | solution.py:24
  22.6 6.9 %collective-permute-start.2 = (f32[2048,16]{0,1:T(8,128)S(1)}, f32[2048,16]{0,1:T(8,128)S(1)}, u32[]{:S(2)}, u32[]{:S(2)}) collective-permute-start(f32[2048,16]{0,1:T(8,128)S(1)} %collective-permute-done), channel_id=1, source_target_pairs={{0,1},{1,2},{2,3},{3,4},{4,5},{5,6},{6,7},{7,8},{8,9},{9,10},{10,1... | collective-permute-start | bytes 393224 | tf_op jit(solution)/shard_map/ppermute | solution.py:19
  24.5 6.9 %collective-permute-start.3 = (f32[2048,16]{0,1:T(8,128)S(1)}, f32[2048,16]{0,1:T(8,128)S(1)}, u32[]{:S(2)}, u32[]{:S(2)}) collective-permute-start(f32[2048,16]{0,1:T(8,128)S(1)} %collective-permute-done.1), channel_id=1, source_target_pairs={{0,15},{1,0},{2,1},{3,2},{4,3},{5,4},{6,5},{7,6},{8,7},{9,8},{10,9... | collective-permute-start | bytes 393224 | tf_op jit(solution)/shard_map/ppermute | solution.py:24
  29.5 6.9 %collective-permute-start.4 = (f32[2048,16]{0,1:T(8,128)S(1)}, f32[2048,16]{0,1:T(8,128)S(1)}, u32[]{:S(2)}, u32[]{:S(2)}) collective-permute-start(f32[2048,16]{0,1:T(8,128)S(1)} %collective-permute-done.2), channel_id=1, source_target_pairs={{0,1},{1,2},{2,3},{3,4},{4,5},{5,6},{6,7},{7,8},{8,9},{9,10},{10,1... | collective-permute-start | bytes 393224 | tf_op jit(solution)/shard_map/ppermute | solution.py:19
  31.4 6.9 %collective-permute-start.5 = (f32[2048,16]{0,1:T(8,128)S(1)}, f32[2048,16]{0,1:T(8,128)S(1)}, u32[]{:S(2)}, u32[]{:S(2)}) collective-permute-start(f32[2048,16]{0,1:T(8,128)S(1)} %collective-permute-done.3), channel_id=1, source_target_pairs={{0,15},{1,0},{2,1},{3,2},{4,3},{5,4},{6,5},{7,6},{8,7},{9,8},{10,9... | collective-permute-start | bytes 393224 | tf_op jit(solution)/shard_map/ppermute | solution.py:24
  36.4 6.9 %collective-permute-start.6 = (f32[2048,16]{0,1:T(8,128)S(1)}, f32[2048,16]{0,1:T(8,128)S(1)}, u32[]{:S(2)}, u32[]{:S(2)}) collective-permute-start(f32[2048,16]{0,1:T(8,128)S(1)} %collective-permute-done.4), channel_id=1, source_target_pairs={{0,1},{1,2},{2,3},{3,4},{4,5},{5,6},{6,7},{7,8},{8,9},{9,10},{10,1... | collective-permute-start | bytes 393224 | tf_op jit(solution)/shard_map/ppermute | solution.py:19
  38.3 6.9 %collective-permute-start.7 = (f32[2048,16]{0,1:T(8,128)S(1)}, f32[2048,16]{0,1:T(8,128)S(1)}, u32[]{:S(2)}, u32[]{:S(2)}) collective-permute-start(f32[2048,16]{0,1:T(8,128)S(1)} %collective-permute-done.5), channel_id=1, source_target_pairs={{0,15},{1,0},{2,1},{3,2},{4,3},{5,4},{6,5},{7,6},{8,7},{9,8},{10,9... | collective-permute-start | bytes 393224 | tf_op jit(solution)/shard_map/ppermute | solution.py:24
  43.3 6.9 %collective-permute-start.8 = (f32[2048,16]{0,1:T(8,128)S(1)}, f32[2048,16]{0,1:T(8,128)S(1)}, u32[]{:S(2)}, u32[]{:S(2)}) collective-permute-start(f32[2048,16]{0,1:T(8,128)S(1)} %collective-permute-done.6), channel_id=1, source_target_pairs={{0,1},{1,2},{2,3},{3,4},{4,5},{5,6},{6,7},{7,8},{8,9},{9,10},{10,1... | collective-permute-start | bytes 393224 | tf_op jit(solution)/shard_map/ppermute | solution.py:19
  45.3 6.9 %collective-permute-start.9 = (f32[2048,16]{0,1:T(8,128)S(1)}, f32[2048,16]{0,1:T(8,128)S(1)}, u32[]{:S(2)}, u32[]{:S(2)}) collective-permute-start(f32[2048,16]{0,1:T(8,128)S(1)} %collective-permute-done.7), channel_id=1, source_target_pairs={{0,15},{1,0},{2,1},{3,2},{4,3},{5,4},{6,5},{7,6},{8,7},{9,8},{10,9... | collective-permute-start | bytes 393224 | tf_op jit(solution)/shard_map/ppermute | solution.py:24
  50.2 6.9 %collective-permute-start.10 = (f32[2048,16]{0,1:T(8,128)S(1)}, f32[2048,16]{0,1:T(8,128)S(1)}, u32[]{:S(2)}, u32[]{:S(2)}) collective-permute-start(f32[2048,16]{0,1:T(8,128)S(1)} %collective-permute-done.8), channel_id=1, source_target_pairs={{0,1},{1,2},{2,3},{3,4},{4,5},{5,6},{6,7},{7,8},{8,9},{9,10},{10,1... | collective-permute-start | bytes 393224 | tf_op jit(solution)/shard_map/ppermute | solution.py:19
  52.2 6.9 %collective-permute-start.11 = (f32[2048,16]{0,1:T(8,128)S(1)}, f32[2048,16]{0,1:T(8,128)S(1)}, u32[]{:S(2)}, u32[]{:S(2)}) collective-permute-start(f32[2048,16]{0,1:T(8,128)S(1)} %collective-permute-done.9), channel_id=1, source_target_pairs={{0,15},{1,0},{2,1},{3,2},{4,3},{5,4},{6,5},{7,6},{8,7},{9,8},{10,9... | collective-permute-start | bytes 393224 | tf_op jit(solution)/shard_map/ppermute | solution.py:24
  57.2 7.7 %collective-permute-start.12 = (f32[2048,16]{0,1:T(8,128)S(1)}, f32[2048,16]{0,1:T(8,128)S(1)}, u32[]{:S(2)}, u32[]{:S(2)}) collective-permute-start(f32[2048,16]{0,1:T(8,128)S(1)} %collective-permute-done.10), channel_id=1, source_target_pairs={{0,1},{1,2},{2,3},{3,4},{4,5},{5,6},{6,7},{7,8},{8,9},{9,10},{10,1... | collective-permute-start | bytes 393224 | tf_op jit(solution)/shard_map/ppermute | solution.py:19
  59.1 7.7 %collective-permute-start.13 = (f32[2048,16]{0,1:T(8,128)S(1)}, f32[2048,16]{0,1:T(8,128)S(1)}, u32[]{:S(2)}, u32[]{:S(2)}) collective-permute-start(f32[2048,16]{0,1:T(8,128)S(1)} %collective-permute-done.11), channel_id=1, source_target_pairs={{0,15},{1,0},{2,1},{3,2},{4,3},{5,4},{6,5},{7,6},{8,7},{9,8},{10,9... | collective-permute-start | bytes 393224 | tf_op jit(solution)/shard_map/ppermute | solution.py:24
  64.8 8.1 %collective-permute-start.14 = (f32[2048,16]{0,1:T(8,128)S(1)}, f32[2048,16]{0,1:T(8,128)S(1)}, u32[]{:S(2)}, u32[]{:S(2)}) collective-permute-start(f32[2048,16]{0,1:T(8,128)S(1)} %collective-permute-done.12), channel_id=1, source_target_pairs={{0,1},{1,2},{2,3},{3,4},{4,5},{5,6},{6,7},{7,8},{8,9},{9,10},{10,1... | collective-permute-start | bytes 393224 | tf_op jit(solution)/shard_map/ppermute | solution.py:19
  72.9 2.6 copy-start
  242.7 39.6 %copy-start.3 = (f32[256,256]{1,0:T(8,128)S(1)}, f32[256,256]{1,0:T(8,128)}, u32[]{:S(2)}) copy-start(f32[256,256]{1,0:T(8,128)} %get-tuple-element.20) | copy-start | bytes 786436
  283.3 2.2 copy-start.2
  284.3 1.6 copy-start.1
Sparse Core Ops, SparseCore 0:
  78.2 140.5 all-reduce.3
